TPU v7x, 32 devices: a whole 2x2x4 slice. The times are simulated.
32 devices in a mesh: dp: 4 (over x, core), expert: 8 (over z, y).
Axes of the slice: x: 2, y: 2, z: 4, core: 2. Of those that a mesh axis runs over, the one named last changes fastest.
Arguments:
- inputs: bfloat16 [512, 4096], P(('dp', 'expert')), may hold values from -6 to 6
- grad_out: bfloat16 [512, 4096], P(('dp', 'expert')), may hold values from -0.796875 to 0.796875
- labels: int32 [512, 1], P(('dp', 'expert')), may hold values from 0 to 7; in each aligned block of 16 rows (0 to 15, 16 to 31, ...) at most 3 rows name the same one
- w_gate: bfloat16 [4096, 57344], P('dp', 'expert'), may hold values from -0.09375 to 0.09375
- w_up: bfloat16 [4096, 57344], P('dp', 'expert'), may hold values from -0.09375 to 0.09375
- w_down: bfloat16 [57344, 4096], P('expert', 'dp'), may hold values from -0.0625 to 0.0625
Outputs:
- grad_in: bfloat16 [512, 4096], P(('dp', 'expert'))
- grad_gate: bfloat16 [4096, 57344], P('dp', 'expert')
- grad_up: bfloat16 [4096, 57344], P('dp', 'expert')
- grad_down: bfloat16 [57344, 4096], P('expert', 'dp')
Inputs may be any that keep to these rules, and one draw needn't show every extreme that they name: `labels`: among the 16 rows of one device no expert is named by more than 3 rows, a bound that some block reaches.
All inputs are finite; a program needn't handle non-finite values.
Results may differ from a plain program's by a relative error of at most 0.011.
Values may be sent and summed in bfloat16 or wider, within the bound.
No kernel may reach another device: no remote copies, remote signals or barrier semaphores. Data moves between devices by JAX's collectives and lax.ppermute only.
A program may use at most 192 MiB of HBM per device.

v0:
```python
import jax
import jax.numpy as jnp
from jax import lax
from jax.sharding import PartitionSpec as P

EXPERTS = 8
ALL = ("dp", "expert")
CHUNKS = 2
LINK = jnp.float32


def nonlinear(gate, up, dhid):
    sig = jax.nn.sigmoid(gate)
    act = gate * sig
    hidden = (act * up).astype(jnp.bfloat16)
    d_up = (dhid * act).astype(jnp.bfloat16)
    d_gate = (dhid * up * sig * (1.0 + gate * (1.0 - sig))).astype(jnp.bfloat16)
    return (hidden, d_up, d_gate)


def contract_rows(left, right):
    return lax.dot_general(
        left, right, (((0,), (0,)), ((), ())), preferred_element_type=jnp.float32
    )


def on_device(inputs, grad_out, labels, w_gate, w_up, w_down):
    members = lax.axis_size("expert")
    replicas = lax.axis_size("dp")
    group = members // EXPERTS
    tok_count = inputs.shape[0]
    width = inputs.shape[1]
    columns = width // replicas
    capacity = 3 * tok_count // (2 * EXPERTS)
    label_col = labels[:, 0]
    onehot = (label_col[:, None] == jnp.arange(EXPERTS, dtype=jnp.int32)[None, :]).astype(jnp.int32)
    before = jnp.cumsum(onehot, axis=0) - onehot
    rank_in = jnp.sum(before * onehot, axis=1)
    slot_ids = label_col * capacity + rank_in
    both = jnp.stack([inputs, grad_out])
    slots = jnp.zeros((2, EXPERTS * capacity, width), jnp.bfloat16).at[:, slot_ids].set(both)
    send = slots.reshape(2, EXPERTS, capacity, replicas, columns)
    send = jnp.transpose(send, (3, 1, 0, 2, 4))
    send = jnp.broadcast_to(
        send[:, :, None], (replicas, EXPERTS, group, 2, capacity, columns)
    ).reshape(replicas * members, 2 * capacity * columns)
    recv = lax.all_to_all(send, ALL, 0, 0, tiled=True)
    recv = recv.reshape(replicas * members, 2, capacity, columns)
    rows_in = recv[:, 0].reshape(-1, columns)
    rows_grad = recv[:, 1].reshape(-1, columns)
    ff = w_gate.shape[1]
    step = ff // CHUNKS
    d_rows = None
    grads = ([], [], [])
    for k in range(CHUNKS):
        cols = slice(k * step, (k + 1) * step)
        g_mat, u_mat, d_mat = (w_gate[:, cols], w_up[:, cols], w_down[cols, :])
        gate_part = jnp.dot(rows_in, g_mat, preferred_element_type=jnp.float32)
        up_part = jnp.dot(rows_in, u_mat, preferred_element_type=jnp.float32)
        dhid_part = lax.dot_general(
            rows_grad, d_mat, (((1,), (1,)), ((), ())), preferred_element_type=jnp.float32
        )
        parts = jnp.stack([gate_part, up_part, dhid_part]).astype(LINK)
        reduced = lax.psum_scatter(parts, "dp", scatter_dimension=2, tiled=True)
        reduced = reduced.astype(jnp.float32)
        hidden, d_up, d_gate = nonlinear(reduced[0], reduced[1], reduced[2])
        gathered = lax.all_gather(jnp.stack([hidden, d_up, d_gate]), "dp", axis=2, tiled=True)
        hidden, d_up, d_gate = (gathered[0], gathered[1], gathered[2])
        part_rows = lax.dot_general(
            d_gate, g_mat, (((1,), (1,)), ((), ())), preferred_element_type=jnp.float32
        ) + lax.dot_general(
            d_up, u_mat, (((1,), (1,)), ((), ())), preferred_element_type=jnp.float32
        )
        d_rows = part_rows if d_rows is None else d_rows + part_rows
        grads[0].append(contract_rows(rows_in, d_gate).astype(jnp.bfloat16))
        grads[1].append(contract_rows(rows_in, d_up).astype(jnp.bfloat16))
        grads[2].append(contract_rows(hidden, rows_grad).astype(jnp.bfloat16))
    back = d_rows.astype(jnp.bfloat16).reshape(replicas * members, capacity * columns)
    back = lax.all_to_all(back, ALL, 0, 0, tiled=True)
    back = back.reshape(replicas, EXPERTS, group, capacity, columns).astype(jnp.float32)
    summed = jnp.sum(back, axis=2)
    summed = jnp.transpose(summed, (1, 2, 0, 3)).reshape(EXPERTS * capacity, width)
    grad_in = summed[slot_ids].astype(jnp.bfloat16)
    grad_gate = jnp.concatenate(grads[0], axis=1)
    grad_up = jnp.concatenate(grads[1], axis=1)
    grad_down = jnp.concatenate(grads[2], axis=0)
    return (grad_in, grad_gate, grad_up, grad_down)


def solution(mesh):
    return jax.shard_map(
        on_device,
        mesh=mesh,
        in_specs=(
            P(ALL, None),
            P(ALL, None),
            P(ALL, None),
            P("dp", "expert"),
            P("dp", "expert"),
            P("expert", "dp"),
        ),
        out_specs=(P(ALL, None), P("dp", "expert"), P("dp", "expert"), P("expert", "dp")),
        check_vma=False,
    )
```

profile of v0, /device:TPU:0, one launch (start us, length us, event | category | flops | bytes accessed | tf_op | source)
XLA Modules:
  0.0 294.1 jit_solution(2347005948940509694)
XLA Ops:
  13.8 2.9 %reduce.3 = bf16[32,6144]{1,0:T(8,128)(2,1)S(1)} reduce(bf16[32,1,6144]{2,1,0:T(2,128)(2,1)S(1)} %all_to_all.16, bf16[]{:T(256)} %broadcast.61), dimensions={1}, to_apply=%all_to_all.16.reduce_sub_computation | reduce | bytes 786434 | tf_op jit(solution)/shard_map/all_to_all | solution.py:47
  17.0 21.0 %all_to_all.20 = bf16[32,2,3072]{2,1,0:T(2,128)(2,1)S(1)} all-to-all(bf16[32,2,3072]{2,1,0:T(2,128)(2,1)S(1)} %reshape.66), channel_id=1, replica_groups=mesh['dp'=4,'expert'=8] {'dp','expert'}, dimensions={0} | all-to-all | bytes 786432 | tf_op jit(solution)/shard_map/all_to_all | solution.py:47
  38.4 2.3 reduce
  41.6 4.4 %fusion.26 = f32[1,96,3584]{2,1,0:T(8,128)S(1)} fusion(bf16[96,1024]{1,0:T(8,128)(2,1)S(1)} %reshape_squeeze.6, bf16[1024,7168]{1,0:T(8,128)(2,1)} %param.9), kind=kOutput, calls=%fused_computation.33 | convolution fusion | flops 704643072 | bytes 8912896 | tf_op jit(solution)/shard_map/dot_general | solution.py:58
  46.0 4.4 %fusion.29 = f32[1,96,3584]{2,1,0:T(8,128)S(1)} fusion(bf16[96,1024]{1,0:T(8,128)(2,1)S(1)} %reshape_squeeze.6, bf16[1024,7168]{1,0:T(8,128)(2,1)} %param.10), kind=kOutput, calls=%fused_computation.34 | convolution fusion | flops 704643072 | bytes 8912896 | tf_op jit(solution)/shard_map/dot_general | solution.py:59
  50.6 5.4 %fusion.35 = f32[1,96,3584]{2,1,0:T(8,128)S(1)} fusion(bf16[96,1024]{1,0:T(8,128)(2,1)S(1)} %reshape_squeeze.7, bf16[7168,1024]{1,0:T(8,128)(2,1)} %param.11), kind=kOutput, calls=%fused_computation.36 | convolution fusion | flops 704643072 | bytes 8912896 | tf_op jit(solution)/shard_map/dot_general | solution.py:60
  58.3 4.4 %fusion.20 = f32[1,96,3584]{2,1,0:T(8,128)S(1)} fusion(bf16[96,1024]{1,0:T(8,128)(2,1)S(1)} %reshape_squeeze.6, bf16[1024,7168]{1,0:T(8,128)(2,1)} %param.9), kind=kOutput, calls=%fused_computation.31 | convolution fusion | flops 704643072 | bytes 8912896 | tf_op jit(solution)/shard_map/dot_general | solution.py:58
  62.7 5.6 %fusion.23 = f32[1,96,3584]{2,1,0:T(8,128)S(1)} fusion(bf16[96,1024]{1,0:T(8,128)(2,1)S(1)} %reshape_squeeze.6, bf16[1024,7168]{1,0:T(8,128)(2,1)} %param.10), kind=kOutput, calls=%fused_computation.32 | convolution fusion | flops 704643072 | bytes 8912896 | tf_op jit(solution)/shard_map/dot_general | solution.py:59
  68.3 5.4 %fusion.32 = f32[1,96,3584]{2,1,0:T(8,128)S(1)} fusion(bf16[96,1024]{1,0:T(8,128)(2,1)S(1)} %reshape_squeeze.7, bf16[7168,1024]{1,0:T(8,128)(2,1)} %param.11), kind=kOutput, calls=%fused_computation.35 | convolution fusion | flops 704643072 | bytes 8912896 | tf_op jit(solution)/shard_map/dot_general | solution.py:60
  76.1 24.1 %reduce-scatter.5.cloned.1.call-done = f32[3,96,896]{2,1,0:T(8,128)} async-done(((f32[3,96,3584]{2,1,0:T(8,128)}), f32[3,96,896]{2,1,0:T(8,128)}) %reduce-scatter.5.cloned.1.call-update) | async-done | bytes 1032208 | tf_op jit(solution)/shard_map/reduce_scatter | solution.py:64
  102.5 12.2 %all-gather.3.cloned.1.call-start = ((), (), s32[]{:S(2)}) async-start(), calls=%async_computation.5 | async-start | bytes 2580480 | tf_op jit(solution)/shard_map/all_gather | solution.py:67
  114.6 33.1 %reduce-scatter.3.cloned.1.call-done = f32[3,96,896]{2,1,0:T(8,128)} async-done(((f32[3,96,3584]{2,1,0:T(8,128)}), f32[3,96,896]{2,1,0:T(8,128)}) %reduce-scatter.3.cloned.1.call-update) | async-done | bytes 1032208 | tf_op jit(solution)/shard_map/reduce_scatter | solution.py:64
  150.0 22.3 %all-gather.5.cloned.1.call-done = bf16[3,96,3584]{2,1,0:T(8,128)(2,1)} async-done(((bf16[3,96,896]{2,1,0:T(8,128)(2,1)}), bf16[3,96,3584]{2,1,0:T(8,128)(2,1)}) %all-gather.5.cloned.1.call-update) | async-done | bytes 2064400 | tf_op jit(solution)/shard_map/all_gather | solution.py:67
  172.3 5.6 %fusion.4 = f32[96,1024]{1,0:T(8,128)S(1)} fusion(bf16[1024,7168]{1,0:T(8,128)(2,1)} %param.10, bf16[3,96,3584]{2,1,0:T(8,128)(2,1)} %all-gather.5.cloned.1.call-done), kind=kOutput, calls=%fused_computation.15 | convolution fusion | flops 704643072 | bytes 8421376 | tf_op jit(solution)/shard_map/dot_general | solution.py:71
  177.9 18.8 %all-gather.3.cloned.1.call-done = bf16[3,96,3584]{2,1,0:T(8,128)(2,1)} async-done(((bf16[3,96,896]{2,1,0:T(8,128)(2,1)}), bf16[3,96,3584]{2,1,0:T(8,128)(2,1)}) %all-gather.3.cloned.1.call-update) | async-done | bytes 2064400 | tf_op jit(solution)/shard_map/all_gather | solution.py:67
  196.7 5.6 %fusion.12 = f32[96,1024]{1,0:T(8,128)S(1)} fusion(bf16[1024,7168]{1,0:T(8,128)(2,1)} %param.10, bf16[3,96,3584]{2,1,0:T(8,128)(2,1)} %all-gather.3.cloned.1.call-done), kind=kOutput, calls=%fused_computation.23 | convolution fusion | flops 704643072 | bytes 8421376 | tf_op jit(solution)/shard_map/dot_general | solution.py:71
  202.4 5.8 %fusion.38 = f32[96,1024]{1,0:T(8,128)S(1)} fusion(f32[96,1024]{1,0:T(8,128)S(1)} %fusion.12, bf16[1024,7168]{1,0:T(8,128)(2,1)} %param.9, bf16[3,96,3584]{2,1,0:T(8,128)(2,1)} %all-gather.3.cloned.1.call-done), kind=kOutput, calls=%fused_computation.39 | convolution fusion | flops 704741376 | bytes 8814592 | tf_op jit(solution)/shard_map/dot_general | solution.py:69
  208.1 5.4 %fusion.47 = bf16[96,1024]{1,0:T(8,128)(2,1)S(1)} fusion(f32[96,1024]{1,0:T(8,128)S(1)} %fusion.38, f32[96,1024]{1,0:T(8,128)S(1)} %fusion.4, bf16[1024,7168]{1,0:T(8,128)(2,1)} %param.9, bf16[3,96,3584]{2,1,0:T(8,128)(2,1)S(1)} %copy-done), kind=kOutput, calls=%fused_computation.42 | convolution fusion | flops 704937984 | bytes 9011200 | tf_op jit(solution)/shard_map/dot_general | solution.py:69
  216.3 4.7 %all-to-all-start.1 = ((bf16[32,2,1536]{2,1,0:T(2,128)(2,1)}), bf16[32,2,1536]{2,1,0:T(2,128)(2,1)}, u32[]{:S(2)}, u32[]{:S(2)}) async-start(bf16[32,2,1536]{2,1,0:T(2,128)(2,1)} %reshape.68), calls=%async_computation.3 | async-start | bytes 393216 | tf_op jit(solution)/shard_map/all_to_all | solution.py:79
  223.2 5.2 %convolution_convert_fusion.4 = bf16[1024,3584]{1,0:T(8,128)(2,1)} fusion(bf16[96,1024]{1,0:T(8,128)(2,1)S(1)} %reshape_squeeze.6, bf16[3,96,3584]{2,1,0:T(8,128)(2,1)S(1)} %copy-done), kind=kOutput, calls=%fused_computation.9 | convolution fusion | flops 708313088 | bytes 8224768 | tf_op jit(solution)/shard_map/dot_general | solution.py:22
  228.3 5.1 %convolution_convert_fusion.3 = bf16[1024,3584]{1,0:T(8,128)(2,1)} fusion(bf16[96,1024]{1,0:T(8,128)(2,1)S(1)} %reshape_squeeze.6, bf16[3,96,3584]{2,1,0:T(8,128)(2,1)S(1)} %copy-done.1), kind=kOutput, calls=%fused_computation.8 | convolution fusion | flops 708313088 | bytes 8224768 | tf_op jit(solution)/shard_map/dot_general | solution.py:22
  233.5 5.1 %convolution_convert_fusion.5 = bf16[1024,3584]{1,0:T(8,128)(2,1)} fusion(bf16[96,1024]{1,0:T(8,128)(2,1)S(1)} %reshape_squeeze.6, bf16[3,96,3584]{2,1,0:T(8,128)(2,1)S(1)} %copy-done.1), kind=kOutput, calls=%fused_computation.10 | convolution fusion | flops 708313088 | bytes 8224768 | tf_op jit(solution)/shard_map/dot_general | solution.py:22
  238.5 18.4 %pad_maximum_fusion = (bf16[1024,7168]{1,0:T(8,128)(2,1)}, bf16[1024,7168]{1,0:T(8,128)(2,1)}) fusion(bf16[1024,3584]{1,0:T(8,128)(2,1)} %convolution_convert_fusion.4, bf16[1024,3584]{1,0:T(8,128)(2,1)} %convolution_convert_fusion.5, bf16[1024,3584]{1,0:T(8,128)(2,1)S(1)} %convolution_convert_fusion.2, bf16[1024,3584]{1,0:T(8,128)(2,1)} %convolution_convert_fusion.3), kind=kLoop, calls=%fused_computation.2 | loop fusion | flops 58720256 | bytes 58720256 | tf_op jit(solution)/shard_map/concatenate | solution.py:84
  261.1 21.7 %pad_maximum_fusion.2 = bf16[7168,1024]{1,0:T(8,128)(2,1)} fusion(bf16[3584,1024]{1,0:T(8,128)(2,1)S(1)} %convolution_convert_fusion, bf16[3584,1024]{1,0:T(8,128)(2,1)S(1)} %convolution_convert_fusion.1), kind=kLoop, calls=%fused_computation.4 | loop fusion | flops 29360128 | bytes 29360128 | tf_op jit(solution)/shard_map/concatenate | solution.py:86
  (51 shorter events, 30.9 us)
Async XLA Ops:
  7.2 93.1 %reduce-scatter.5.cloned.1.call-start = ((), (), s32[]{:S(2)}) async-start(), calls=%async_computation.6 | async-start | bytes 5160960 | tf_op jit(solution)/shard_map/reduce_scatter | solution.py:64
  58.3 89.4 %reduce-scatter.3.cloned.1.call-start = ((), (), s32[]{:S(2)}) async-start(), calls=%async_computation.4 | async-start | bytes 5160960 | tf_op jit(solution)/shard_map/reduce_scatter | solution.py:64
  76.0 96.3 %all-gather.5.cloned.1.call-start = ((), (), s32[]{:S(2)}) async-start(), calls=%async_computation.7 | async-start | bytes 2580480 | tf_op jit(solution)/shard_map/all_gather | solution.py:67
  102.5 94.2 %all-gather.3.cloned.1.call-start = ((), (), s32[]{:S(2)}) async-start(), calls=%async_computation.5 | async-start | bytes 2580480 | tf_op jit(solution)/shard_map/all_gather | solution.py:67
  202.4 5.8 %copy-start = (bf16[3,96,3584]{2,1,0:T(8,128)(2,1)S(1)}, bf16[3,96,3584]{2,1,0:T(8,128)(2,1)}, u32[]{:S(2)}) copy-start(bf16[3,96,3584]{2,1,0:T(8,128)(2,1)} %all-gather.5.cloned.1.call-done) | copy-start | bytes 6193156
  216.3 66.5 %all-to-all-start.1 = ((bf16[32,2,1536]{2,1,0:T(2,128)(2,1)}), bf16[32,2,1536]{2,1,0:T(2,128)(2,1)}, u32[]{:S(2)}, u32[]{:S(2)}) async-start(bf16[32,2,1536]{2,1,0:T(2,128)(2,1)} %reshape.68), calls=%async_computation.3 | async-start | bytes 393216 | tf_op jit(solution)/shard_map/all_to_all | solution.py:79
  223.2 5.2 %copy-start.1 = (bf16[3,96,3584]{2,1,0:T(8,128)(2,1)S(1)}, bf16[3,96,3584]{2,1,0:T(8,128)(2,1)}, u32[]{:S(2)}) copy-start(bf16[3,96,3584]{2,1,0:T(8,128)(2,1)} %all-gather.3.cloned.1.call-done) | copy-start | bytes 6193156
  256.9 2.1 copy-start.2
Sparse Core Ops, SparseCore 0:
  58.4 41.7 reduce-scatter.4
  103.5 44.1 reduce-scatter.2
  149.9 22.3 all-gather.4
  174.3 22.3 all-gather.2
where the time goes:
time: 299 us; the launch traced here: 294 us
  waiting for transfers between devices  98.4 us (33%)
  matrix products  73.7 us (25%)
  other arithmetic  60.4 us (20%)
  blocking collectives  21 us (7%)
  starting transfers between devices  17 us (6%)
  between operations  14.3 us (5%)
  local copies, waits for them, and re-layouts  9.31 us (3%)
    reduce_scatter x2, waiting for transfers between devices, on_device(): reduced = lax.psum_scatter(parts, 'dp', scatter_dimension=2, tiled=True)  57.2 us
    all_gather x2, waiting for transfers between devices, on_device(): lax.all_gather(jnp.stack([hidden, d_up, d_gate]), 'dp', axis=2, tiled=True)  41.1 us
    concatenate x1, other arithmetic, on_device(): grad_down = jnp.concatenate(grads[2], axis=0)  21.7 us
    dot_general x6, matrix products, contract_rows(): lax.dot_general(left, right, (((0,), (0,)), ((), ())), preferred_element_...  21.6 us
    all_to_all x1, blocking collectives, on_device(): recv = lax.all_to_all(send, ALL, 0, 0, tiled=True)  21 us
    concatenate x1, other arithmetic, on_device(): grad_gate = jnp.concatenate(grads[0], axis=1)  18.4 us
    all_gather x2, starting transfers between devices, on_device(): lax.all_gather(jnp.stack([hidden, d_up, d_gate]), 'dp', axis=2, tiled=True)  12.2 us
    dot_general x2, matrix products, on_device(): lax.dot_general(d_up, u_mat, (((1,), (1,)), ((), ())), preferred_element_...  11.3 us
  transfers between devices with their start and end apart: 5, of which 4 were waited for; matrix products, arithmetic and copies ran while one was open for 30% of the time, Pallas kernels for 0%

commit v1 on v0

--- a/solution.py
+++ b/solution.py
@@ -64,7 +64,24 @@
         reduced = lax.psum_scatter(parts, "dp", scatter_dimension=2, tiled=True)
         reduced = reduced.astype(jnp.float32)
         hidden, d_up, d_gate = nonlinear(reduced[0], reduced[1], reduced[2])
-        gathered = lax.all_gather(jnp.stack([hidden, d_up, d_gate]), "dp", axis=2, tiled=True)
+        x = jnp.stack([hidden, d_up, d_gate])
+        ways, here, lap = (lax.axis_size("dp"), lax.axis_index("dp"), x.shape[2])
+        shape = [n * ways if d == 2 else n for d, n in enumerate(x.shape)]
+        full = lax.dynamic_update_slice_in_dim(jnp.zeros(shape, x.dtype), x, here * lap, axis=2)
+        going_up = going_down = x
+        for far in range(1, ways // 2 + 1):
+            going_up = lax.ppermute(going_up, "dp", [(d, (d + 1) % ways) for d in range(ways)])
+            full = lax.dynamic_update_slice_in_dim(
+                full, going_up, (here - far) % ways * lap, axis=2
+            )
+            if 2 * far < ways:
+                going_down = lax.ppermute(
+                    going_down, "dp", [(d, (d - 1) % ways) for d in range(ways)]
+                )
+                full = lax.dynamic_update_slice_in_dim(
+                    full, going_down, (here + far) % ways * lap, axis=2
+                )
+        gathered = full
         hidden, d_up, d_gate = (gathered[0], gathered[1], gathered[2])
         part_rows = lax.dot_general(
             d_gate, g_mat, (((1,), (1,)), ((), ())), preferred_element_type=jnp.float32

time: 299 us -> 284 us (0.950)
  waiting for transfers between devices: 98.4 us -> 88 us
  starting transfers between devices: 17 us -> 8.62 us
  other arithmetic: 60.4 us -> 52.8 us
  local copies, waits for them, and re-layouts: 9.31 us -> 16.4 us
  matrix products: 73.7 us -> 77.7 us
    all_gather x2 -> x0, waiting for transfers between devices: 41.1 us -> none  [on_device(): lax.all_gather(jnp.stack([hidden, d_up, d_gate]), 'dp', axis=2, tiled=True)]
    ppermute x0 -> x6, waiting for transfers between devices: none -> 20 us  [the longest x4 11.4 us: on_device(): lax.ppermute(going_up, 'dp', [(d, (d + 1) % ways) for d in range(ways)])]
    dot_general x6, matrix products: 21.6 us -> 34.3 us  [contract_rows(): lax.dot_general(left, right, (((0,), (0,)), ((), ())), preferred_element_...]
    all_gather x2 -> x0, starting transfers between devices: 12.2 us -> none  [on_device(): lax.all_gather(jnp.stack([hidden, d_up, d_gate]), 'dp', axis=2, tiled=True)]
    concatenate x1, other arithmetic: 21.7 us -> 10.3 us  [on_device(): grad_down = jnp.concatenate(grads[2], axis=0)]
    reduce_scatter x2, waiting for transfers between devices: 57.2 us -> 68 us  [on_device(): reduced = lax.psum_scatter(parts, 'dp', scatter_dimension=2, tiled=True)]
    dynamic_update_slice x0 -> x6, local copies, waits for them, and re-layouts: none -> 5.95 us  [the longest x2 3.12 us: on_device(): lax.dynamic_update_slice_in_dim(full, going_down, (here + far) % ways * l...]
    dot_general x2, matrix products: 11.2 us -> 5.88 us  [on_device(): lax.dot_general(d_gate, g_mat, (((1,), (1,)), ((), ())), preferred_elemen...]
  transfers between devices with their start and end apart: 5 -> 9, of which waited for: 4 -> 4; matrix products, arithmetic and copies ran while one was open for 30% -> 26% of each run, Pallas kernels for 0% -> 0%
where the time goes in v1:
time: 284 us; the launch traced here: 279 us
  waiting for transfers between devices  88 us (31%)
  matrix products  77.7 us (27%)
  other arithmetic  52.8 us (19%)
  blocking collectives  21.1 us (7%)
  local copies, waits for them, and re-layouts  16.4 us (6%)
  between operations  14.6 us (5%)
  starting transfers between devices  8.62 us (3%)
    reduce_scatter x2, waiting for transfers between devices, on_device(): reduced = lax.psum_scatter(parts, 'dp', scatter_dimension=2, tiled=True)  68 us
    dot_general x6, matrix products, contract_rows(): lax.dot_general(left, right, (((0,), (0,)), ((), ())), preferred_element_...  34.3 us
    all_to_all x1, blocking collectives, on_device(): recv = lax.all_to_all(send, ALL, 0, 0, tiled=True)  21.1 us
    concatenate x1, other arithmetic, on_device(): grad_gate = jnp.concatenate(grads[0], axis=1)  21.1 us
    ppermute x4, waiting for transfers between devices, on_device(): lax.ppermute(going_up, 'dp', [(d, (d + 1) % ways) for d in range(ways)])  11.4 us
    dot_general x2, matrix products, on_device(): lax.dot_general(rows_grad, d_mat, (((1,), (1,)), ((), ())), preferred_ele...  10.9 us
    concatenate x1, other arithmetic, on_device(): grad_down = jnp.concatenate(grads[2], axis=0)  10.3 us
    dot_general x2, matrix products, on_device(): up_part = jnp.dot(rows_in, u_mat, preferred_element_type=jnp.float32)  9.67 us
  transfers between devices with their start and end apart: 9, of which 4 were waited for; matrix products, arithmetic and copies ran while one was open for 26% of the time, Pallas kernels for 0%

profile of v1, /device:TPU:0, one launch (start us, length us, event | category | flops | bytes accessed | tf_op | source)
XLA Modules:
  0.0 279.2 jit_solution(1094300652591555925)
XLA Ops:
  13.8 2.9 %reduce.3 = bf16[32,6144]{1,0:T(8,128)(2,1)S(1)} reduce(bf16[32,1,6144]{2,1,0:T(2,128)(2,1)S(1)} %all_to_all.16, bf16[]{:T(256)} %broadcast.68), dimensions={1}, to_apply=%all_to_all.16.reduce_sub_computation | reduce | bytes 786434 | tf_op jit(solution)/shard_map/all_to_all | solution.py:47
  17.0 21.1 %all_to_all.20 = bf16[32,2,3072]{2,1,0:T(2,128)(2,1)S(1)} all-to-all(bf16[32,2,3072]{2,1,0:T(2,128)(2,1)S(1)} %reshape.66), channel_id=1, replica_groups=mesh['dp'=4,'expert'=8] {'dp','expert'}, dimensions={0} | all-to-all | bytes 786432 | tf_op jit(solution)/shard_map/all_to_all | solution.py:47
  41.9 4.4 %fusion.29 = f32[1,96,3584]{2,1,0:T(8,128)S(1)} fusion(bf16[96,1024]{1,0:T(8,128)(2,1)S(1)} %reshape_squeeze.6, bf16[1024,7168]{1,0:T(8,128)(2,1)} %param.10), kind=kOutput, calls=%fused_computation.34 | convolution fusion | flops 704643072 | bytes 8912896 | tf_op jit(solution)/shard_map/dot_general | solution.py:59
  46.3 4.4 %fusion.26 = f32[1,96,3584]{2,1,0:T(8,128)S(1)} fusion(bf16[96,1024]{1,0:T(8,128)(2,1)S(1)} %reshape_squeeze.6, bf16[1024,7168]{1,0:T(8,128)(2,1)} %param.9), kind=kOutput, calls=%fused_computation.33 | convolution fusion | flops 704643072 | bytes 8912896 | tf_op jit(solution)/shard_map/dot_general | solution.py:58
  50.7 5.5 %fusion.35 = f32[1,96,3584]{2,1,0:T(8,128)S(1)} fusion(bf16[96,1024]{1,0:T(8,128)(2,1)S(1)} %reshape_squeeze.7, bf16[7168,1024]{1,0:T(8,128)(2,1)} %param.11), kind=kOutput, calls=%fused_computation.36 | convolution fusion | flops 704643072 | bytes 8912896 | tf_op jit(solution)/shard_map/dot_general | solution.py:60
  58.5 5.5 %fusion.32 = f32[1,96,3584]{2,1,0:T(8,128)S(1)} fusion(bf16[96,1024]{1,0:T(8,128)(2,1)S(1)} %reshape_squeeze.7, bf16[7168,1024]{1,0:T(8,128)(2,1)} %param.11), kind=kOutput, calls=%fused_computation.35 | convolution fusion | flops 704643072 | bytes 8912896 | tf_op jit(solution)/shard_map/dot_general | solution.py:60
  63.9 5.3 %fusion.23 = f32[1,96,3584]{2,1,0:T(8,128)S(1)} fusion(bf16[96,1024]{1,0:T(8,128)(2,1)S(1)} %reshape_squeeze.6, bf16[1024,7168]{1,0:T(8,128)(2,1)} %param.10), kind=kOutput, calls=%fused_computation.32 | convolution fusion | flops 704643072 | bytes 8912896 | tf_op jit(solution)/shard_map/dot_general | solution.py:59
  69.2 4.4 %fusion.20 = f32[1,96,3584]{2,1,0:T(8,128)S(1)} fusion(bf16[96,1024]{1,0:T(8,128)(2,1)S(1)} %reshape_squeeze.6, bf16[1024,7168]{1,0:T(8,128)(2,1)} %param.9), kind=kOutput, calls=%fused_computation.31 | convolution fusion | flops 704643072 | bytes 8912896 | tf_op jit(solution)/shard_map/dot_general | solution.py:58
  75.9 24.4 %reduce-scatter.5.cloned.1.call-done = f32[3,96,896]{2,1,0:T(8,128)} async-done(((f32[3,96,3584]{2,1,0:T(8,128)}), f32[3,96,896]{2,1,0:T(8,128)}) %reduce-scatter.5.cloned.1.call-update) | async-done | bytes 1032208 | tf_op jit(solution)/shard_map/reduce_scatter | solution.py:64
  104.2 43.6 %reduce-scatter.3.cloned.1.call-done = f32[3,96,896]{2,1,0:T(8,128)} async-done(((f32[3,96,3584]{2,1,0:T(8,128)}), f32[3,96,896]{2,1,0:T(8,128)}) %reduce-scatter.3.cloned.1.call-update) | async-done | bytes 1032208 | tf_op jit(solution)/shard_map/reduce_scatter | solution.py:64
  152.5 11.4 %collective-permute-done = bf16[3,96,896]{2,1,0:T(8,128)(2,1)S(1)} collective-permute-done((bf16[3,96,896]{2,1,0:T(8,128)(2,1)}, bf16[3,96,896]{2,1,0:T(8,128)(2,1)S(1)}, u32[]{:S(2)}, u32[]{:S(2)}) %collective-permute-start) | collective-permute-done | bytes 516128 | tf_op jit(solution)/shard_map/ppermute | solution.py:73
  167.0 8.5 %collective-permute-done.1 = bf16[3,96,896]{2,1,0:T(8,128)(2,1)} collective-permute-done((bf16[3,96,896]{2,1,0:T(8,128)(2,1)}, bf16[3,96,896]{2,1,0:T(8,128)(2,1)}, u32[]{:S(2)}, u32[]{:S(2)}) %collective-permute-start.1) | collective-permute-done | bytes 516128 | tf_op jit(solution)/shard_map/ppermute | solution.py:78
  178.6 6.4 %convolution_convert_fusion.4 = bf16[1024,3584]{1,0:T(8,128)(2,1)} fusion(bf16[96,1024]{1,0:T(8,128)(2,1)S(1)} %reshape_squeeze.6, bf16[3,96,3584]{2,1,0:T(8,128)(2,1)} %constant_dynamic-update-slice_fusion.7), kind=kOutput, calls=%fused_computation.9 | convolution fusion | flops 708313088 | bytes 8224768 | tf_op jit(solution)/shard_map/dot_general | solution.py:22
  185.0 5.8 %fusion.4 = f32[96,1024]{1,0:T(8,128)S(1)} fusion(bf16[1024,7168]{1,0:T(8,128)(2,1)} %param.10, bf16[3,96,3584]{2,1,0:T(8,128)(2,1)} %constant_dynamic-update-slice_fusion.7), kind=kOutput, calls=%fused_computation.15 | convolution fusion | flops 704643072 | bytes 8421376 | tf_op jit(solution)/shard_map/dot_general | solution.py:88
  193.3 5.0 %convolution_convert_fusion.5 = bf16[1024,3584]{1,0:T(8,128)(2,1)} fusion(bf16[96,1024]{1,0:T(8,128)(2,1)S(1)} %reshape_squeeze.6, bf16[3,96,3584]{2,1,0:T(8,128)(2,1)S(1)} %constant_dynamic-update-slice_fusion.3), kind=kOutput, calls=%fused_computation.10 | convolution fusion | flops 708313088 | bytes 8224768 | tf_op jit(solution)/shard_map/dot_general | solution.py:22
  198.3 6.2 %convolution_convert_fusion.2 = bf16[1024,3584]{1,0:T(8,128)(2,1)} fusion(bf16[96,1024]{1,0:T(8,128)(2,1)S(1)} %reshape_squeeze.6, bf16[3,96,3584]{2,1,0:T(8,128)(2,1)} %constant_dynamic-update-slice_fusion.7), kind=kOutput, calls=%fused_computation.7 | convolution fusion | flops 708313088 | bytes 8224768 | tf_op jit(solution)/shard_map/dot_general | solution.py:22
  204.5 5.0 %convolution_convert_fusion.3 = bf16[1024,3584]{1,0:T(8,128)(2,1)} fusion(bf16[96,1024]{1,0:T(8,128)(2,1)S(1)} %reshape_squeeze.6, bf16[3,96,3584]{2,1,0:T(8,128)(2,1)S(1)} %constant_dynamic-update-slice_fusion.3), kind=kOutput, calls=%fused_computation.8 | convolution fusion | flops 708313088 | bytes 8224768 | tf_op jit(solution)/shard_map/dot_general | solution.py:22
  209.5 6.5 %convolution_convert_fusion = bf16[3584,1024]{1,0:T(8,128)(2,1)} fusion(bf16[96,1024]{1,0:T(8,128)(2,1)S(1)} %reshape_squeeze.7, bf16[3,96,3584]{2,1,0:T(8,128)(2,1)} %constant_dynamic-update-slice_fusion.7), kind=kOutput, calls=%fused_computation.5 | convolution fusion | flops 708313088 | bytes 8224768 | tf_op jit(solution)/shard_map/dot_general | solution.py:22
  216.1 5.0 %convolution_convert_fusion.1 = bf16[3584,1024]{1,0:T(8,128)(2,1)} fusion(bf16[96,1024]{1,0:T(8,128)(2,1)S(1)} %reshape_squeeze.7, bf16[3,96,3584]{2,1,0:T(8,128)(2,1)S(1)} %constant_dynamic-update-slice_fusion.3), kind=kOutput, calls=%fused_computation.6 | convolution fusion | flops 708313088 | bytes 8224768 | tf_op jit(solution)/shard_map/dot_general | solution.py:22
  221.1 3.5 %fusion.41 = f32[96,1024]{1,0:T(8,128)S(1)} fusion(f32[96,1024]{1,0:T(8,128)S(1)} %fusion.4, bf16[1024,7168]{1,0:T(8,128)(2,1)S(1)} %bitcast.79, bf16[3,96,3584]{2,1,0:T(8,128)(2,1)} %constant_dynamic-update-slice_fusion.7), kind=kOutput, calls=%fused_computation.40 | convolution fusion | flops 704741376 | bytes 8814592 | tf_op jit(solution)/shard_map/dot_general | solution.py:86
  227.2 2.6 reduce.4
  231.6 6.1 %all-to-all-start.1 = ((bf16[32,2,1536]{2,1,0:T(2,128)(2,1)}), bf16[32,2,1536]{2,1,0:T(2,128)(2,1)S(1)}, u32[]{:S(2)}, u32[]{:S(2)}) async-start(bf16[32,2,1536]{2,1,0:T(2,128)(2,1)} %reshape.68), calls=%async_computation.3 | async-start | bytes 393216 | tf_op jit(solution)/shard_map/all_to_all | solution.py:96
  237.7 21.1 %pad_maximum_fusion = (bf16[1024,7168]{1,0:T(8,128)(2,1)}, bf16[1024,7168]{1,0:T(8,128)(2,1)}) fusion(bf16[1024,3584]{1,0:T(8,128)(2,1)} %convolution_convert_fusion.4, bf16[1024,3584]{1,0:T(8,128)(2,1)} %convolution_convert_fusion.5, bf16[1024,3584]{1,0:T(8,128)(2,1)} %convolution_convert_fusion.2, bf16[1024,3584]{1,0:T(8,128)(2,1)} %convolution_convert_fusion.3), kind=kLoop, calls=%fused_computation.2 | loop fusion | flops 58720256 | bytes 58720256 | tf_op jit(solution)/shard_map/concatenate | solution.py:101
  258.8 10.3 %pad_maximum_fusion.2 = bf16[7168,1024]{1,0:T(8,128)(2,1)} fusion(bf16[3584,1024]{1,0:T(8,128)(2,1)S(1)} %bitcast.67, bf16[3584,1024]{1,0:T(8,128)(2,1)} %convolution_convert_fusion.1), kind=kLoop, calls=%fused_computation.4 | loop fusion | flops 29360128 | bytes 29360128 | tf_op jit(solution)/shard_map/concatenate | solution.py:103
  (82 shorter events, 39.6 us)
Async XLA Ops:
  7.2 93.2 %reduce-scatter.5.cloned.1.call-start = ((), (), s32[]{:S(2)}) async-start(), calls=%async_computation.5 | async-start | bytes 5160960 | tf_op jit(solution)/shard_map/reduce_scatter | solution.py:64
  58.4 89.4 %reduce-scatter.3.cloned.1.call-start = ((), (), s32[]{:S(2)}) async-start(), calls=%async_computation.4 | async-start | bytes 5160960 | tf_op jit(solution)/shard_map/reduce_scatter | solution.py:64
  104.2 47.8 %collective-permute-start.3 = (bf16[3,96,896]{2,1,0:T(8,128)(2,1)}, bf16[3,96,896]{2,1,0:T(8,128)(2,1)S(1)}, u32[]{:S(2)}, u32[]{:S(2)}) collective-permute-start(bf16[3,96,896]{2,1,0:T(8,128)(2,1)} %get-tuple-element.14), channel_id=1, source_target_pairs={{0,8},{8,16},{16,24},{24,0},{1,9},{9,17},{17,25},{25,1},{2,10},{10... | collective-permute-start | bytes 1548296 | tf_op jit(solution)/shard_map/ppermute | solution.py:73
  150.2 13.7 %collective-permute-start = (bf16[3,96,896]{2,1,0:T(8,128)(2,1)}, bf16[3,96,896]{2,1,0:T(8,128)(2,1)S(1)}, u32[]{:S(2)}, u32[]{:S(2)}) collective-permute-start(bf16[3,96,896]{2,1,0:T(8,128)(2,1)} %get-tuple-element.12), channel_id=1, source_target_pairs={{0,8},{8,16},{16,24},{24,0},{1,9},{9,17},{17,25},{25,1},{2,10},{10... | collective-permute-start | bytes 1548296 | tf_op jit(solution)/shard_map/ppermute | solution.py:73
  150.2 14.8 %collective-permute-start.4 = (bf16[3,96,896]{2,1,0:T(8,128)(2,1)}, bf16[3,96,896]{2,1,0:T(8,128)(2,1)}, u32[]{:S(2)}, u32[]{:S(2)}) collective-permute-start(bf16[3,96,896]{2,1,0:T(8,128)(2,1)} %get-tuple-element.14), channel_id=1, source_target_pairs={{0,24},{8,0},{16,8},{24,16},{1,25},{9,1},{17,9},{25,17},{2,26},{10... | collective-permute-start | bytes 1548296 | tf_op jit(solution)/shard_map/ppermute | solution.py:78
  152.0 23.6 %collective-permute-start.1 = (bf16[3,96,896]{2,1,0:T(8,128)(2,1)}, bf16[3,96,896]{2,1,0:T(8,128)(2,1)}, u32[]{:S(2)}, u32[]{:S(2)}) collective-permute-start(bf16[3,96,896]{2,1,0:T(8,128)(2,1)} %get-tuple-element.12), channel_id=1, source_target_pairs={{0,24},{8,0},{16,8},{24,16},{1,25},{9,1},{17,9},{25,17},{2,26},{10... | collective-permute-start | bytes 1548296 | tf_op jit(solution)/shard_map/ppermute | solution.py:78
  152.0 24.7 %collective-permute-start.5 = (bf16[3,96,896]{2,1,0:T(8,128)(2,1)S(1)}, bf16[3,96,896]{2,1,0:T(8,128)(2,1)}, u32[]{:S(2)}, u32[]{:S(2)}) collective-permute-start(bf16[3,96,896]{2,1,0:T(8,128)(2,1)S(1)} %collective-permute-done.3), channel_id=1, source_target_pairs={{0,8},{8,16},{16,24},{24,0},{1,9},{9,17},{17,25},{25,1},{2,10},{10... | collective-permute-start | bytes 1548296 | tf_op jit(solution)/shard_map/ppermute | solution.py:73
  163.9 26.8 %collective-permute-start.2 = (bf16[3,96,896]{2,1,0:T(8,128)(2,1)S(1)}, bf16[3,96,896]{2,1,0:T(8,128)(2,1)S(1)}, u32[]{:S(2)}, u32[]{:S(2)}) collective-permute-start(bf16[3,96,896]{2,1,0:T(8,128)(2,1)S(1)} %collective-permute-done), channel_id=1, source_target_pairs={{0,8},{8,16},{16,24},{24,0},{1,9},{9,17},{17,25},{25,1},{2,10},{10... | collective-permute-start | bytes 1548296 | tf_op jit(solution)/shard_map/ppermute | solution.py:73
  164.9 25.9 %slice-start.2 = ((s8[14680064]{0:T(1024)(128)(4,1)}), s8[4194304]{0:T(1024)(128)(4,1)S(1)}, s32[]{:S(2)}) async-start(s8[14680064]{0:T(1024)(128)(4,1)} %bitcast.76), calls=%async_computation.8 | async-start | bytes 8388608
  178.6 12.3 %slice-start.3 = ((s8[14680064]{0:T(1024)(128)(4,1)}), s8[4194304]{0:T(1024)(128)(4,1)S(1)}, s32[]{:S(2)}) async-start(s8[14680064]{0:T(1024)(128)(4,1)} %bitcast.76), calls=%async_computation.9 | async-start | bytes 8388608
  178.6 12.3 %slice-start.4 = ((s8[14680064]{0:T(1024)(128)(4,1)}), s8[4194304]{0:T(1024)(128)(4,1)S(1)}, s32[]{:S(2)}) async-start(s8[14680064]{0:T(1024)(128)(4,1)} %bitcast.76), calls=%async_computation.10 | async-start | bytes 8388608
  185.0 5.9 %slice-start.5 = ((s8[14680064]{0:T(1024)(128)(4,1)}), s8[2097152]{0:T(1024)(128)(4,1)S(1)}, s32[]{:S(2)}) async-start(s8[14680064]{0:T(1024)(128)(4,1)} %bitcast.76), calls=%async_computation.11 | async-start | bytes 4194304
  204.5 16.6 %slice-start.6 = ((s8[14680064]{0:T(1024)(128)(4,1)}), s8[4194304]{0:T(1024)(128)(4,1)S(1)}, s32[]{:S(2)}) async-start(s8[14680064]{0:T(1024)(128)(4,1)} %bitcast.78), calls=%async_computation.12 | async-start | bytes 8388608
  204.5 16.6 %slice-start.7 = ((s8[14680064]{0:T(1024)(128)(4,1)}), s8[4194304]{0:T(1024)(128)(4,1)S(1)}, s32[]{:S(2)}) async-start(s8[14680064]{0:T(1024)(128)(4,1)} %bitcast.78), calls=%async_computation.13 | async-start | bytes 8388608
  209.5 11.6 %slice-start.8 = ((s8[14680064]{0:T(1024)(128)(4,1)}), s8[4194304]{0:T(1024)(128)(4,1)S(1)}, s32[]{:S(2)}) async-start(s8[14680064]{0:T(1024)(128)(4,1)} %bitcast.78), calls=%async_computation.14 | async-start | bytes 8388608
  216.1 5.0 %slice-start.9 = ((s8[14680064]{0:T(1024)(128)(4,1)}), s8[2097152]{0:T(1024)(128)(4,1)S(1)}, s32[]{:S(2)}) async-start(s8[14680064]{0:T(1024)(128)(4,1)} %bitcast.78), calls=%async_computation.15 | async-start | bytes 4194304
  227.2 31.6 %slice-start = ((s8[7340032]{0:T(1024)(128)(4,1)}), s8[3145728]{0:T(1024)(128)(4,1)S(1)}, s32[]{:S(2)}) async-start(s8[7340032]{0:T(1024)(128)(4,1)} %bitcast.66), calls=%async_computation.6 | async-start | bytes 6291456
  231.6 37.5 %all-to-all-start.1 = ((bf16[32,2,1536]{2,1,0:T(2,128)(2,1)}), bf16[32,2,1536]{2,1,0:T(2,128)(2,1)S(1)}, u32[]{:S(2)}, u32[]{:S(2)}) async-start(bf16[32,2,1536]{2,1,0:T(2,128)(2,1)} %reshape.68), calls=%async_computation.3 | async-start | bytes 393216 | tf_op jit(solution)/shard_map/all_to_all | solution.py:96
  237.7 21.1 %slice-start.1 = ((s8[7340032]{0:T(1024)(128)(4,1)}), s8[4194304]{0:T(1024)(128)(4,1)S(1)}, s32[]{:S(2)}) async-start(s8[7340032]{0:T(1024)(128)(4,1)} %bitcast.66), calls=%async_computation.7 | async-start | bytes 8388608
Sparse Core Ops, SparseCore 0:
  58.5 41.7 reduce-scatter.4
  103.7 44.0 reduce-scatter.2
